TPU v7x, 128 devices: a whole 4x4x4 slice. The times are simulated.
128 devices in a mesh: kz: 4 (over x_hi, core), en: 32 (over z, y, x_lo).
Axes of the slice: x: 4 (x_hi: 2, x_lo: 2; x = x_hi * 2 + x_lo), y: 4, z: 4, core: 2. Of those that a mesh axis runs over, the one named last changes fastest.
Arguments:
- sigma_less: bfloat16 [4, 128, 3, 2, 128, 128], P('kz', 'en'), as said below
- sigma_great: bfloat16 [4, 128, 3, 2, 128, 128], P('kz', 'en'), as said below
- onsite_table: float32 [3, 128, 128], replicated, as said below
- cos_coupling: float32 [3, 128, 128], replicated, as said below
- slab_coupling: float32 [2, 128, 128], replicated, may hold values from -0.25 to 0.25
- slab_kind: int32 [3], replicated, may hold values from 0 to 2, as said below
- kz_table: int32 [4, 4], replicated, may hold values from 0 to 3, as said below
- mode_weight: float32 [2, 4], replicated, may hold values from 0.25 to 2
- form_factor: float32 [2, 128, 128], replicated, as said below
- occupation: float32 [2], replicated, may hold values from 0.1 to 2
- energy_offset: int32 [2], replicated, may hold values from 1 to 4, as said below
Outputs:
- sigma_less_new: bfloat16 [4, 128, 3, 2, 128, 128], P('kz', 'en')
- sigma_great_new: bfloat16 [4, 128, 3, 2, 128, 128], P('kz', 'en')
Inputs may be any that keep to these rules, and one draw needn't show every extreme that they name: `sigma_less`: each block is i times a Hermitian matrix. `sigma_great`: each block is -i times a Hermitian matrix. `onsite_table`: each block is symmetric. `cos_coupling`: each block is symmetric. `form_factor`: each block is symmetric and positive. `kz_table`: each row names every momentum once. `slab_kind`: every kind is used by some slab. `energy_offset`: the modes have different offsets, and some mode has exactly 4.
All inputs are finite; a program needn't handle non-finite values.
Results may differ from a plain program's by a relative error of at most 0.0029.
Values may be sent and summed in bfloat16 or wider, within the bound.
No kernel may reach another device: no remote copies, remote signals or barrier semaphores. Data moves between devices by JAX's collectives and lax.ppermute only.
A program may use at most 128 MiB of HBM per device.

v0:
```python
import jax
import jax.numpy as jnp
from jax import lax
from jax.sharding import PartitionSpec as P

OFFMAX = 4
DAMPING = 0.3


def padded(block, sides, width):
    for axis, dim in sides:
        count = lax.axis_size(axis)
        forward = [(i, i + 1) for i in range(count - 1)]
        backward = [(target, source) for source, target in forward]
        low = lax.ppermute(
            lax.slice_in_dim(block, block.shape[dim] - width, None, axis=dim), axis, forward
        )
        high = lax.ppermute(lax.slice_in_dim(block, 0, width, axis=dim), axis, backward)
        block = jnp.concatenate([low, block, high], axis=dim)
    return block


def matmul_high(left_matrix, right_matrix):
    return jnp.matmul(left_matrix, right_matrix, precision=lax.Precision.HIGHEST)


def complex_product(left_pair, right_pair):
    real_part = matmul_high(left_pair[0], right_pair[0]) - matmul_high(left_pair[1], right_pair[1])
    imag_part = matmul_high(left_pair[0], right_pair[1]) + matmul_high(left_pair[1], right_pair[0])
    return (real_part, imag_part)


def real_left(matrix, pair_value):
    return (matmul_high(matrix, pair_value[0]), matmul_high(matrix, pair_value[1]))


def real_right(pair_value, matrix):
    return (matmul_high(pair_value[0], matrix), matmul_high(pair_value[1], matrix))


def adjoint(pair_value):
    return (jnp.swapaxes(pair_value[0], -1, -2), -jnp.swapaxes(pair_value[1], -1, -2))


def add_pair(left_pair, right_pair):
    return (left_pair[0] + right_pair[0], left_pair[1] + right_pair[1])


def sub_pair(left_pair, right_pair):
    return (left_pair[0] - right_pair[0], left_pair[1] - right_pair[1])


def invert_pair(pair_value):
    orbitals = pair_value[0].shape[-1]
    upper_half = jnp.concatenate([pair_value[0], -pair_value[1]], axis=-1)
    lower_half = jnp.concatenate([pair_value[1], pair_value[0]], axis=-1)
    embedded = jnp.concatenate([upper_half, lower_half], axis=-2)
    transposed = jnp.swapaxes(embedded, -1, -2)
    normal = matmul_high(transposed, embedded)
    factor = jnp.linalg.cholesky(normal)
    solved = jax.scipy.linalg.cho_solve((factor, True), transposed)
    return (solved[..., :orbitals, :orbitals], solved[..., orbitals:, :orbitals])


def greater_of(less_pair, ret_pair):
    return sub_pair(add_pair(less_pair, ret_pair), adjoint(ret_pair))


def pack_pair(pair_value):
    return jnp.stack([pair_value[0], pair_value[1]], axis=-3)


def green_blocks(sigma_less, sigma_great, hamilton, slab_coupling, energies):
    orbitals = sigma_less.shape[-1]
    slab_count = sigma_less.shape[2]
    identity = jnp.eye(orbitals, dtype=jnp.float32)
    energy_grid = energies[None, :, None, None]
    left_ret = []
    left_less = []
    for slab_index in range(slab_count):
        lesser = sigma_less[:, :, slab_index].astype(jnp.float32)
        greater = sigma_great[:, :, slab_index].astype(jnp.float32)
        retarded_re = 0.5 * (greater[:, :, 0] - lesser[:, :, 0])
        retarded_im = 0.5 * (greater[:, :, 1] - lesser[:, :, 1]) - DAMPING * identity
        system_re = energy_grid * identity - hamilton[:, :, slab_index] - retarded_re
        system_im = -retarded_im
        source = (lesser[:, :, 0], lesser[:, :, 1])
        if slab_index > 0:
            coupling = slab_coupling[slab_index - 1]
            folded = real_right(real_left(coupling, left_ret[-1]), coupling.T)
            system_re = system_re - folded[0]
            system_im = system_im - folded[1]
            source = add_pair(source, real_right(real_left(coupling, left_less[-1]), coupling.T))
        inverse = invert_pair((system_re, system_im))
        left_ret.append(inverse)
        left_less.append(complex_product(complex_product(inverse, source), adjoint(inverse)))
    full_ret = left_ret[-1]
    full_less = left_less[-1]
    lesser_list = [full_less]
    greater_list = [greater_of(full_less, full_ret)]
    for slab_index in range(slab_count - 2, -1, -1):
        coupling = slab_coupling[slab_index]
        green_couple = real_right(left_ret[slab_index], coupling)
        bridge = real_right(complex_product(green_couple, full_ret), coupling.T)
        cross_term = complex_product(bridge, left_less[slab_index])
        spread = complex_product(
            real_right(complex_product(green_couple, full_less), coupling.T),
            adjoint(left_ret[slab_index]),
        )
        full_less = add_pair(
            add_pair(left_less[slab_index], spread), sub_pair(cross_term, adjoint(cross_term))
        )
        full_ret = add_pair(left_ret[slab_index], complex_product(bridge, left_ret[slab_index]))
        lesser_list.insert(0, full_less)
        greater_list.insert(0, greater_of(full_less, full_ret))
    lesser_all = jnp.stack([pack_pair(item) for item in lesser_list], axis=2)
    greater_all = jnp.stack([pack_pair(item) for item in greater_list], axis=2)
    return jnp.stack([lesser_all, greater_all], axis=2).astype(jnp.bfloat16)


def hamiltonian(onsite_table, cos_coupling, slab_kind, momenta_index, momenta_total):
    kind_count = onsite_table.shape[0]
    choose = (slab_kind[:, None] == jnp.arange(kind_count, dtype=jnp.int32)[None, :]).astype(
        jnp.float32
    )
    onsite = jnp.einsum("sk,kij->sij", choose, onsite_table, precision=lax.Precision.HIGHEST)
    phase_factor = jnp.cos(2.0 * jnp.pi * momenta_index.astype(jnp.float32) / momenta_total)
    hamilton = onsite[None] + phase_factor[:, None, None, None] * cos_coupling[None]
    return hamilton[:, None]


def momentum_weights(table_rows, mode_weight, momenta_total):
    onehot = (
        table_rows[:, :, None] == jnp.arange(momenta_total, dtype=jnp.int32)[None, None, :]
    ).astype(jnp.float32)
    return (
        jnp.einsum("lq,aqk->lak", mode_weight, onehot, precision=lax.Precision.HIGHEST)
        / momenta_total
    )


def mixed_sums(extended, weights, form_factor, occupation, energy_offset, energy_count, margin):
    total_less = None
    total_great = None
    for mode_index in range(form_factor.shape[0]):
        shift_steps = energy_offset[mode_index]
        upper_side = lax.dynamic_slice_in_dim(extended, margin + shift_steps, energy_count, 1)
        lower_side = lax.dynamic_slice_in_dim(extended, margin - shift_steps, energy_count, 1)
        occupied = occupation[mode_index]
        less_term = (occupied + 1.0) * upper_side[:, :, 0].astype(
            jnp.float32
        ) + occupied * lower_side[:, :, 0].astype(jnp.float32)
        great_term = (occupied + 1.0) * lower_side[:, :, 1].astype(
            jnp.float32
        ) + occupied * upper_side[:, :, 1].astype(jnp.float32)
        less_sum = form_factor[mode_index] * jnp.einsum(
            "ak,kesrij->aesrij", weights[mode_index], less_term, precision=lax.Precision.HIGHEST
        )
        great_sum = form_factor[mode_index] * jnp.einsum(
            "ak,kesrij->aesrij", weights[mode_index], great_term, precision=lax.Precision.HIGHEST
        )
        total_less = less_sum if total_less is None else total_less + less_sum
        total_great = great_sum if total_great is None else total_great + great_sum
    return (total_less, total_great)


def on_device(
    sigma_less,
    sigma_great,
    onsite_table,
    cos_coupling,
    slab_coupling,
    slab_kind,
    kz_table,
    mode_weight,
    form_factor,
    occupation,
    energy_offset,
):
    momenta_local = sigma_less.shape[0]
    energy_local = sigma_less.shape[1]
    momenta_total = momenta_local * lax.axis_size("kz")
    energy_total = energy_local * lax.axis_size("en")
    momenta_start = lax.axis_index("kz") * momenta_local
    momenta_index = momenta_start + jnp.arange(momenta_local, dtype=jnp.int32)
    energy_index = lax.axis_index("en") * energy_local + jnp.arange(energy_local, dtype=jnp.int32)
    energies = -1.5 + 3.0 * (energy_index.astype(jnp.float32) + 0.5) / energy_total
    hamilton = hamiltonian(onsite_table, cos_coupling, slab_kind, momenta_index, momenta_total)
    blocks = green_blocks(sigma_less, sigma_great, hamilton, slab_coupling, energies)
    table_rows = lax.dynamic_slice_in_dim(kz_table, momenta_start, momenta_local, 0)
    weights = momentum_weights(table_rows, mode_weight, momenta_total)
    everyone = lax.all_gather(blocks, "kz", axis=0, tiled=True)
    extended = padded(everyone, (("en", 1),), OFFMAX)
    less_total, great_total = mixed_sums(
        extended, weights, form_factor, occupation, energy_offset, energy_local, OFFMAX
    )
    return (less_total.astype(jnp.bfloat16), great_total.astype(jnp.bfloat16))


def solution(mesh):
    in_specs = (
        P("kz", "en", None, None, None, None),
        P("kz", "en", None, None, None, None),
        P(),
        P(),
        P(),
        P(),
        P(),
        P(),
        P(),
        P(),
        P(),
    )
    out_specs = (P("kz", "en", None, None, None, None), P("kz", "en", None, None, None, None))
    return jax.shard_map(
        on_device, mesh=mesh, in_specs=in_specs, out_specs=out_specs, check_vma=False
    )
```

profile of v0, /device:TPU:1, one launch (start us, length us, event | category | flops | bytes accessed | tf_op | source)
XLA Modules:
  0.0 1280.6 jit_solution(12174855667015090132)
XLA Ops:
  7.4 2.0 fusion.356
  9.4 2.0 fusion.357
  14.7 1.9 fusion.44
  20.6 47.1 %custom-call.23 = f32[1,4,128,128]{3,2,1,0:T(8,128)S(1)} custom-call(f32[1,4,128,128]{3,2,1,0:T(8,128)S(1)} %cholesky.281), custom_call_target="Cholesky" | custom-call | tf_op jit(solution)/shard_map/jit(cholesky)/cholesky | solution.py:60
  67.7 39.3 %custom-call.24 = f32[1,4,1,128,128]{3,4,2,1,0:T(8,128)S(1)} custom-call(f32[1,4,1,128,128]{4,3,2,1,0:T(8,128)S(1)} %select_bitcast_fusion.2), custom_call_target="InvertDiagBlocksLowerTriangular" | custom-call | tf_op jit(solution)/shard_map/jit(cholesky)/cholesky | solution.py:60
  110.1 46.9 %custom-call.25 = f32[1,4,128,128]{3,2,1,0:T(8,128)S(1)} custom-call(f32[1,4,128,128]{3,2,1,0:T(8,128)S(1)} %fusion.25), custom_call_target="Cholesky" | custom-call | tf_op jit(solution)/shard_map/jit(cholesky)/cholesky | solution.py:60
  159.6 4.1 while.6
  163.7 78.8 %custom-call.26 = f32[4,2,128,128]{2,3,1,0:T(8,128)S(1)} custom-call(f32[4,2,128,128]{3,2,1,0:T(8,128)S(1)} %bitcast.917), custom_call_target="InvertDiagBlocksLowerTriangular" | custom-call | tf_op jit(solution)/shard_map/jit(_cho_solve)/vmap()/triangular_solve | solution.py:61
  258.9 47.3 %custom-call.27 = f32[1,4,128,128]{3,2,1,0:T(8,128)S(1)} custom-call(f32[1,4,128,128]{3,2,1,0:T(8,128)S(1)} %cholesky.284), custom_call_target="Cholesky" | custom-call | tf_op jit(solution)/shard_map/jit(cholesky)/cholesky | solution.py:60
  306.4 39.3 %custom-call.28 = f32[1,4,1,128,128]{3,4,2,1,0:T(8,128)S(1)} custom-call(f32[1,4,1,128,128]{4,3,2,1,0:T(8,128)S(1)} %select_bitcast_fusion.1), custom_call_target="InvertDiagBlocksLowerTriangular" | custom-call | tf_op jit(solution)/shard_map/jit(cholesky)/cholesky | solution.py:60
  348.7 46.9 %custom-call.29 = f32[1,4,128,128]{3,2,1,0:T(8,128)S(1)} custom-call(f32[1,4,128,128]{3,2,1,0:T(8,128)S(1)} %fusion.26), custom_call_target="Cholesky" | custom-call | tf_op jit(solution)/shard_map/jit(cholesky)/cholesky | solution.py:60
  396.2 4.1 while.7
  400.2 78.8 %custom-call.30 = f32[4,2,128,128]{2,3,1,0:T(8,128)S(1)} custom-call(f32[4,2,128,128]{3,2,1,0:T(8,128)S(1)} %bitcast.918), custom_call_target="InvertDiagBlocksLowerTriangular" | custom-call | tf_op jit(solution)/shard_map/jit(_cho_solve)/vmap()/triangular_solve | solution.py:61
  479.1 1.9 fusion.53
  497.9 2.1 fusion.40
  510.8 47.3 %custom-call.31 = f32[1,4,128,128]{3,2,1,0:T(8,128)S(1)} custom-call(f32[1,4,128,128]{3,2,1,0:T(8,128)S(1)} %cholesky.287), custom_call_target="Cholesky" | custom-call | tf_op jit(solution)/shard_map/jit(cholesky)/cholesky | solution.py:60
  561.3 40.8 %custom-call.32 = f32[1,4,1,128,128]{3,4,2,1,0:T(8,128)} custom-call(f32[1,4,1,128,128]{4,3,2,1,0:T(8,128)} %select_bitcast_fusion), custom_call_target="InvertDiagBlocksLowerTriangular" | custom-call | tf_op jit(solution)/shard_map/jit(cholesky)/cholesky | solution.py:60
  603.5 2.3 fusion.27
  605.8 48.4 %custom-call.33 = f32[1,4,128,128]{3,2,1,0:T(8,128)} custom-call(f32[1,4,128,128]{3,2,1,0:T(8,128)} %fusion.27), custom_call_target="Cholesky" | custom-call | tf_op jit(solution)/shard_map/jit(cholesky)/cholesky | solution.py:60
  658.6 6.8 while.8
  659.8 2.1 bitcast_dynamic-update-slice_fusion.11
  663.2 2.1 bitcast_dynamic-update-slice_fusion.11
  665.3 80.2 %custom-call.34 = f32[4,2,128,128]{2,3,1,0:T(8,128)} custom-call(f32[4,2,128,128]{3,2,1,0:T(8,128)} %bitcast.916), custom_call_target="InvertDiagBlocksLowerTriangular" | custom-call | tf_op jit(solution)/shard_map/jit(_cho_solve)/vmap()/triangular_solve | solution.py:61
  745.6 1.8 fusion.51
  792.5 2.0 fusion.32
  796.3 2.2 fusion.17
  800.3 2.0 fusion.33
  808.6 2.4 fusion.370
  819.5 2.3 convolution_subtract_fusion.7
  823.6 2.1 fusion.30
  830.1 2.5 fusion.10
  834.4 2.1 fusion.31
  840.0 1.9 convert_bitcast_fusion.2
  847.5 2.1 convert_bitcast_fusion.5
  849.6 2.0 convert_bitcast_fusion.4
  856.0 54.2 %all-gather.2.cloned.1.call-done = bf16[4,4,2,3,2,128,128]{6,5,4,3,2,1,0:T(8,128)(2,1)} async-done(((bf16[1,4,2,3,2,128,128]{6,5,4,3,2,1,0:T(8,128)(2,1)}), bf16[4,4,2,3,2,128,128]{6,5,4,3,2,1,0:T(8,128)(2,1)}) %all-gather.2.cloned.1.call-update) | async-done | bytes 6291472 | tf_op jit(solution)/shard_map/all_gather | solution.py:192
  910.2 4.9 collective-permute-start
  925.1 122.2 %collective-permute-done = bf16[4,4,2,3,2,128,128]{6,5,4,3,2,1,0:T(8,128)(2,1)} collective-permute-done((bf16[4,4,2,3,2,128,128]{6,5,4,3,2,1,0:T(8,128)(2,1)}, bf16[4,4,2,3,2,128,128]{6,5,4,3,2,1,0:T(8,128)(2,1)}, u32[]{:S(2)}, u32[]{:S(2)}) %collective-permute-start) | collective-permute-done | bytes 6291488 | tf_op jit(solution)/shard_map/ppermute | solution.py:15
  1047.3 8.0 constant_dynamic-update-slice_fusion.2
  1055.3 4.1 constant_dynamic-update-slice_fusion.1
  1059.4 125.6 %collective-permute-done.1 = bf16[4,4,2,3,2,128,128]{6,5,4,3,2,1,0:T(8,128)(2,1)} collective-permute-done((bf16[4,4,2,3,2,128,128]{6,5,4,3,2,1,0:T(8,128)(2,1)}, bf16[4,4,2,3,2,128,128]{6,5,4,3,2,1,0:T(8,128)(2,1)}, u32[]{:S(2)}, u32[]{:S(2)}) %collective-permute-start.1) | collective-permute-done | bytes 6291488 | tf_op jit(solution)/shard_map/ppermute | solution.py:18
  1185.0 8.1 constant_dynamic-update-slice_fusion
  1193.0 18.2 %add_bitcast_fusion.1 = (f32[4,4,3,2,128,128]{5,4,3,2,1,0:T(8,128)S(1)}, f32[4,4,3,2,128,128]{5,4,3,2,1,0:T(8,128)}, f32[4,4,3,2,128,128]{5,4,3,2,1,0:T(8,128)}, f32[4,4,3,2,128,128]{5,4,3,2,1,0:T(8,128)}) fusion(bf16[4,12,2,3,2,128,128]{6,5,4,3,2,1,0:T(8,128)(2,1)} %constant_dynamic-update-slice_fusion, s32[]{:T(128)S(6)} %select_n.19, s32[]{:T(128)S(6)} %add.377, ...), kind=kLoop, calls=%fused_computation.15 | loop fusion | flops 31457280 | bytes 50331684 | tf_op jit(solution)/shard_map/add | solution.py:153
  1211.3 19.0 %fusion.6 = f32[1,4,3,2,128,128]{5,0,4,3,2,1:T(1,128)S(1)} fusion(f32[4,4,3,2,128,128]{5,4,3,2,1,0:T(8,128)} %get-tuple-element.68, f32[2,4]{1,0:T(2,128)S(1)} %fusion.36), kind=kOutput, calls=%fused_computation.12 | convolution fusion | flops 18874368 | bytes 7864832 | tf_op jit(solution)/shard_map/ak,kesrij->aesrij/dot_general | solution.py:156
  1230.2 13.8 %fusion.4 = f32[1,4,3,2,128,128]{5,0,4,3,2,1:T(1,128)S(1)} fusion(f32[4,4,3,2,128,128]{5,4,3,2,1,0:T(8,128)S(1)} %copy-done.3, f32[2,4]{1,0:T(2,128)S(1)} %fusion.36), kind=kOutput, calls=%fused_computation.10 | convolution fusion | flops 18874368 | bytes 7864832 | tf_op jit(solution)/shard_map/ak,kesrij->aesrij/dot_general | solution.py:156
  1244.1 13.6 %fusion.2 = f32[1,4,3,2,128,128]{5,0,4,3,2,1:T(1,128)S(1)} fusion(f32[4,4,3,2,128,128]{5,4,3,2,1,0:T(8,128)S(1)} %get-tuple-element.65, f32[2,4]{1,0:T(2,128)S(1)} %fusion.36), kind=kOutput, calls=%fused_computation.8 | convolution fusion | flops 18874368 | bytes 7864832 | tf_op jit(solution)/shard_map/ak,kesrij->aesrij/dot_general | solution.py:159
  1257.7 13.9 %fusion = f32[1,4,3,2,128,128]{5,0,4,3,2,1:T(1,128)S(1)} fusion(f32[4,4,3,2,128,128]{5,4,3,2,1,0:T(8,128)S(1)} %bitcast.900, f32[2,4]{1,0:T(2,128)S(1)} %fusion.36), kind=kOutput, calls=%fused_computation.6 | convolution fusion | flops 18874368 | bytes 7864832 | tf_op jit(solution)/shard_map/ak,kesrij->aesrij/dot_general | solution.py:159
  1271.6 1.9 fusion.47
  (359 shorter events, 167.4 us)
Async XLA Ops:
  7.2 903.0 %all-gather.2.cloned.1.call-start = ((), (), s32[]{:S(2)}) async-start(), calls=%async_computation | async-start | bytes 7864320 | tf_op jit(solution)/shard_map/all_gather | solution.py:192
  7.3 60.4 %copy-start.56 = (pred[128,128]{1,0:T(8,128)(4,1)}, pred[128,128]{1,0:T(8,128)(4,1)S(1)}, u32[]{:S(2)}) copy-start(pred[128,128]{1,0:T(8,128)(4,1)S(1)} %iota_compare_fusion.1) | copy-start | bytes 49156
  7.4 388.5 %copy-start.36 = (pred[256,256]{1,0:T(8,128)(4,1)}, pred[256,256]{1,0:T(8,128)(4,1)S(1)}, u32[]{:S(2)}) copy-start(pred[256,256]{1,0:T(8,128)(4,1)S(1)} %iota_compare_fusion) | copy-start | bytes 196612
  16.8 233.7 %copy-start.51 = (f32[128,128]{0,1:T(8,128)}, f32[128,128]{0,1:T(8,128)S(1)}, u32[]{:S(2)}) copy-start(f32[128,128]{0,1:T(8,128)S(1)} %copy.266) | copy-start | bytes 196612
  159.6 87.2 %copy-start.2 = (f32[2,128,128]{2,1,0:T(8,128)S(1)}, f32[2,128,128]{2,1,0:T(8,128)}, u32[]{:S(2)}) copy-start(f32[2,128,128]{2,1,0:T(8,128)} %param.18) | copy-start | bytes 393220
  163.7 83.7 %copy-start.63 = (s32[2,2]{1,0:T(2,128)}, s32[2,2]{1,0:T(2,128)S(1)}, u32[]{:S(2)}) copy-start(s32[2,2]{1,0:T(2,128)S(1)} %get-tuple-element.256) | copy-start | bytes 52
  248.1 8.5 copy-start.52
  251.9 54.4 %copy-start.57 = (pred[128,128]{1,0:T(8,128)(4,1)S(1)}, pred[128,128]{1,0:T(8,128)(4,1)}, u32[]{:S(2)}) copy-start(pred[128,128]{1,0:T(8,128)(4,1)} %copy-done.56) | copy-start | bytes 49156
  255.2 140.9 %copy-start.64 = (s32[2,2]{1,0:T(2,128)S(1)}, s32[2,2]{1,0:T(2,128)}, u32[]{:S(2)}) copy-start(s32[2,2]{1,0:T(2,128)} %copy-done.63) | copy-start | bytes 52
  479.1 11.8 copy-start.50
  489.7 13.0 %copy-start.40 = (bf16[1,4,2,128,128]{4,3,1,2,0:T(8,128)(2,1)S(1)}, bf16[1,4,2,128,128]{4,3,1,2,0:T(8,128)(2,1)}, u32[]{:S(2)}) copy-start(bf16[1,4,2,128,128]{4,3,1,2,0:T(8,128)(2,1)} %get-tuple-element.88) | copy-start | bytes 786436
  492.7 12.7 copy-start.29
  745.6 8.9 copy-start.41
  745.6 8.9 copy-start.47
  754.8 8.8 copy-start.30
  755.5 12.4 copy-start.8
  757.6 26.9 %copy-start.10 = (f32[4,128,128]{1,2,0:T(8,128)}, f32[4,128,128]{1,2,0:T(8,128)S(1)}, u32[]{:S(2)}) copy-start(f32[4,128,128]{1,2,0:T(8,128)S(1)} %convolution_subtract_fusion.24) | copy-start | bytes 786436
  759.8 9.2 copy-start.19
  762.5 9.3 copy-start.18
  763.1 25.7 %copy-start.15 = (f32[4,128,128]{1,2,0:T(8,128)}, f32[4,128,128]{1,2,0:T(8,128)S(1)}, u32[]{:S(2)}) copy-start(f32[4,128,128]{1,2,0:T(8,128)S(1)} %convolution_add_fusion.13) | copy-start | bytes 786436
  768.9 13.7 %copy-start.4 = (f32[4,128,128]{2,1,0:T(8,128)}, f32[4,128,128]{2,1,0:T(8,128)S(1)}, u32[]{:S(2)}) copy-start(f32[4,128,128]{2,1,0:T(8,128)S(1)} %fusion.174) | copy-start | bytes 786436
  773.1 10.6 copy-start.16
  774.2 10.4 copy-start.20
  779.7 9.1 copy-start.24
  783.7 11.5 copy-start.5
  800.3 10.7 copy-start.7
  800.3 11.8 copy-start.13
  800.3 11.8 copy-start.34
  802.3 9.8 copy-start.35
  802.4 13.1 %copy-start.17 = (f32[4,128,128]{2,1,0:T(8,128)S(1)}, f32[4,128,128]{2,1,0:T(8,128)}, u32[]{:S(2)}) copy-start(f32[4,128,128]{2,1,0:T(8,128)} %copy-done.16) | copy-start | bytes 786436
  802.4 14.6 %copy-start.14 = (f32[1,4,128,128]{3,2,1,0:T(8,128)S(1)}, f32[1,4,128,128]{3,2,1,0:T(8,128)}, u32[]{:S(2)}) copy-start(f32[1,4,128,128]{3,2,1,0:T(8,128)} %copy-done.12) | copy-start | bytes 786436
  802.4 17.1 %copy-start.9 = (f32[4,128,128]{1,2,0:T(8,128)S(1)}, f32[4,128,128]{1,2,0:T(8,128)}, u32[]{:S(2)}) copy-start(f32[4,128,128]{1,2,0:T(8,128)} %copy-done.8) | copy-start | bytes 786436
  803.7 11.0 copy-start.21
  807.2 22.9 %copy-start.11 = (f32[4,128,128]{1,2,0:T(8,128)S(1)}, f32[4,128,128]{1,2,0:T(8,128)}, u32[]{:S(2)}) copy-start(f32[4,128,128]{1,2,0:T(8,128)} %copy-done.10) | copy-start | bytes 786436
  816.9 23.0 %copy-start.23 = (f32[1,4,128,128]{3,2,1,0:T(8,128)S(1)}, f32[1,4,128,128]{3,2,1,0:T(8,128)}, u32[]{:S(2)}) copy-start(f32[1,4,128,128]{3,2,1,0:T(8,128)} %copy-done.22) | copy-start | bytes 786436
  830.1 22.6 %copy-start.53 = (bf16[1,4,1,128,128]{3,4,1,2,0:T(8,128)(2,1)S(1)}, bf16[1,4,1,128,128]{3,4,1,2,0:T(8,128)(2,1)}, u32[]{:S(2)}) copy-start(bf16[1,4,1,128,128]{3,4,1,2,0:T(8,128)(2,1)} %convert_bitcast_fusion) | copy-start | bytes 393220
  853.7 62.7 %copy-start.60 = (s32[2]{0:T(128)S(1)}, s32[2]{0:T(128)}, u32[]{:S(2)}) copy-start(s32[2]{0:T(128)} %param.24) | copy-start | bytes 28
  853.7 68.5 %copy-start.61 = (f32[2]{0:T(128)S(1)}, f32[2]{0:T(128)}, u32[]{:S(2)}) copy-start(f32[2]{0:T(128)} %param.23) | copy-start | bytes 28
  853.7 71.2 %copy-start.62 = (f32[2,4]{1,0:T(2,128)S(1)}, f32[2,4]{1,0:T(2,128)}, u32[]{:S(2)}) copy-start(f32[2,4]{1,0:T(2,128)} %param.21) | copy-start | bytes 100
  853.8 71.3 %copy-start.58 = (f32[2,128,128]{2,1,0:T(8,128)S(1)}, f32[2,128,128]{2,1,0:T(8,128)}, u32[]{:S(2)}) copy-start(f32[2,128,128]{2,1,0:T(8,128)} %param.22) | copy-start | bytes 393220
  910.2 137.2 %collective-permute-start = (bf16[4,4,2,3,2,128,128]{6,5,4,3,2,1,0:T(8,128)(2,1)}, bf16[4,4,2,3,2,128,128]{6,5,4,3,2,1,0:T(8,128)(2,1)}, u32[]{:S(2)}, u32[]{:S(2)}) collective-permute-start(bf16[4,4,2,3,2,128,128]{6,5,4,3,2,1,0:T(8,128)(2,1)} %all-gather.2.cloned.1.call-done), channel_id=1, source_target_pairs={{0,1},{1,2},{2,3},{3,4},{4,5},{5,6},{6,7},{7,8},{8,9},{9,10},{10,1... | collective-permute-start | bytes 18874376 | tf_op jit(solution)/shard_map/ppermute | solution.py:15
  915.1 269.9 %collective-permute-start.1 = (bf16[4,4,2,3,2,128,128]{6,5,4,3,2,1,0:T(8,128)(2,1)}, bf16[4,4,2,3,2,128,128]{6,5,4,3,2,1,0:T(8,128)(2,1)}, u32[]{:S(2)}, u32[]{:S(2)}) collective-permute-start(bf16[4,4,2,3,2,128,128]{6,5,4,3,2,1,0:T(8,128)(2,1)} %all-gather.2.cloned.1.call-done), channel_id=1, source_target_pairs={{1,0},{2,1},{3,2},{4,3},{5,4},{6,5},{7,6},{8,7},{9,8},{10,9},{11,1... | collective-permute-start | bytes 18874376 | tf_op jit(solution)/shard_map/ppermute | solution.py:18
  925.1 130.3 %slice-start.2 = ((s8[6291456]{0:T(1024)(128)(4,1)}), s8[4194304]{0:T(1024)(128)(4,1)S(1)}, s32[]{:S(2)}) async-start(s8[6291456]{0:T(1024)(128)(4,1)} %bitcast.901), calls=%async_computation.3 | async-start | bytes 8388608
  925.1 130.2 %slice-start.3 = ((s8[6291456]{0:T(1024)(128)(4,1)}), s8[2097152]{0:T(1024)(128)(4,1)S(1)}, s32[]{:S(2)}) async-start(s8[6291456]{0:T(1024)(128)(4,1)} %bitcast.901), calls=%async_computation.4 | async-start | bytes 4194304
  1211.2 19.0 %copy-start.3 = (f32[4,4,3,2,128,128]{5,4,3,2,1,0:T(8,128)S(1)}, f32[4,4,3,2,128,128]{5,4,3,2,1,0:T(8,128)}, u32[]{:S(2)}) copy-start(f32[4,4,3,2,128,128]{5,4,3,2,1,0:T(8,128)} %get-tuple-element.66) | copy-start | bytes 18874372
  1230.2 27.5 %slice-start = ((s8[6291456]{0:T(1024)(128)(4,1)}), s8[4194304]{0:T(1024)(128)(4,1)S(1)}, s32[]{:S(2)}) async-start(s8[6291456]{0:T(1024)(128)(4,1)} %bitcast.899), calls=%async_computation.1 | async-start | bytes 8388608
  1244.1 13.6 %slice-start.1 = ((s8[6291456]{0:T(1024)(128)(4,1)}), s8[2097152]{0:T(1024)(128)(4,1)S(1)}, s32[]{:S(2)}) async-start(s8[6291456]{0:T(1024)(128)(4,1)} %bitcast.899), calls=%async_computation.2 | async-start | bytes 4194304
  1257.7 15.8 %copy-start.1 = (f32[3,128,128]{2,1,0:T(8,128)S(1)}, f32[3,128,128]{2,1,0:T(8,128)}, u32[]{:S(2)}) copy-start(f32[3,128,128]{2,1,0:T(8,128)} %param.16) | copy-start | bytes 589828
  (24 other events, 91.1 us)
Sparse Core Ops, SparseCore 0:
  856.1 54.0 all-gather.1
where the time goes:
time: 1290 us; the launch traced here: 1280 us
  other arithmetic  684 us (53%)
  waiting for transfers between devices  302 us (23%)
  matrix products  181 us (14%)
  local copies, waits for them, and re-layouts  83.6 us (6%)
  between operations  22.8 us (2%)
    another operation x26, other arithmetic, invert_pair(): factor = jnp.linalg.cholesky(normal)  407 us
    another operation x8, other arithmetic, invert_pair(): solved = jax.scipy.linalg.cho_solve((factor, True), transposed)  241 us
    ppermute x1, waiting for transfers between devices, padded(): lax.ppermute(lax.slice_in_dim(block, 0, width, axis=dim), axis, backward)  126 us
    ppermute x1, waiting for transfers between devices, padded(): lax.ppermute(lax.slice_in_dim(block, block.shape[dim] - width, None, axis...  122 us
    dot_general x95, matrix products, matmul_high(): jnp.matmul(left_matrix, right_matrix, precision=lax.Precision.HIGHEST)  89.9 us
    all_gather x1, waiting for transfers between devices, on_device(): everyone = lax.all_gather(blocks, 'kz', axis=0, tiled=True)  54.2 us
    dot_general x2, matrix products, mixed_sums(): jnp.einsum('ak,kesrij->aesrij', weights[mode_index], less_term, precision...  32.8 us
    dot_general x2, matrix products, mixed_sums(): jnp.einsum('ak,kesrij->aesrij', weights[mode_index], great_term, precisio...  27.5 us
  transfers between devices with their start and end apart: 3, of which 3 were waited for; matrix products, arithmetic and copies ran while one was open for 1% of the time, Pallas kernels for 0%

commit v1 on v0

--- a/solution.py
+++ b/solution.py
@@ -5,6 +5,11 @@
 
 OFFMAX = 4
 DAMPING = 0.3
+
+
+def all_by_exchange(x, axis, along):
+    sent = jnp.stack([x] * lax.axis_size(axis))
+    return jnp.concatenate(lax.all_to_all(sent, axis, 0, 0), axis=along)
 
 
 def padded(block, sides, width):
@@ -189,7 +194,7 @@
     blocks = green_blocks(sigma_less, sigma_great, hamilton, slab_coupling, energies)
     table_rows = lax.dynamic_slice_in_dim(kz_table, momenta_start, momenta_local, 0)
     weights = momentum_weights(table_rows, mode_weight, momenta_total)
-    everyone = lax.all_gather(blocks, "kz", axis=0, tiled=True)
+    everyone = all_by_exchange(blocks, "kz", 0)
     extended = padded(everyone, (("en", 1),), OFFMAX)
     less_total, great_total = mixed_sums(
         extended, weights, form_factor, occupation, energy_offset, energy_local, OFFMAX

time: 1290 us -> 1320 us (1.023)
  blocking collectives: 0 us -> 76.9 us
  waiting for transfers between devices: 302 us -> 259 us
  other arithmetic: 684 us -> 710 us
  local copies, waits for them, and re-layouts: 83.6 us -> 67.5 us
  between operations: 22.8 us -> 9.37 us
    all_to_all x0 -> x1, blocking collectives: none -> 76.9 us  [all_by_exchange(): return jnp.concatenate(lax.all_to_all(sent, axis, 0, 0), axis=along)]
    all_gather x1 -> x0, waiting for transfers between devices: 54.2 us -> none  [on_device(): everyone = lax.all_gather(blocks, 'kz', axis=0, tiled=True)]
    concatenate x0 -> x1, other arithmetic: none -> 15 us  [padded(): block = jnp.concatenate([low, block, high], axis=dim)]
  transfers between devices with their start and end apart: 3 -> 2, of which waited for: 3 -> 2; matrix products, arithmetic and copies ran while one was open for 1% -> 0% of each run, Pallas kernels for 0% -> 0%
where the time goes in v1:
time: 1320 us
  other arithmetic  710 us (54%)
  waiting for transfers between devices  259 us (20%)
  matrix products  188 us (14%)
  blocking collectives  76.9 us (6%)
  local copies, waits for them, and re-layouts  67.5 us (5%)
    another operation x26, other arithmetic, invert_pair(): factor = jnp.linalg.cholesky(normal)  411 us
    another operation x8, other arithmetic, invert_pair(): solved = jax.scipy.linalg.cho_solve((factor, True), transposed)  243 us
    ppermute x1, waiting for transfers between devices, padded(): lax.ppermute(lax.slice_in_dim(block, 0, width, axis=dim), axis, backward)  137 us
    ppermute x1, waiting for transfers between devices, padded(): lax.ppermute(lax.slice_in_dim(block, block.shape[dim] - width, None, axis...  121 us
    dot_general x95, matrix products, matmul_high(): jnp.matmul(left_matrix, right_matrix, precision=lax.Precision.HIGHEST)  96.6 us
    all_to_all x1, blocking collectives, all_by_exchange(): return jnp.concatenate(lax.all_to_all(sent, axis, 0, 0), axis=along)  76.9 us
    dot_general x2, matrix products, mixed_sums(): jnp.einsum('ak,kesrij->aesrij', weights[mode_index], less_term, precision...  32.8 us
    dot_general x2, matrix products, mixed_sums(): jnp.einsum('ak,kesrij->aesrij', weights[mode_index], great_term, precisio...  27.5 us
  transfers between devices with their start and end apart: 2, of which 2 were waited for; matrix products, arithmetic and copies ran while one was open for 0% of the time, Pallas kernels for 0%

profile of v1, /device:TPU:1, one launch (start us, length us, event | category | flops | bytes accessed | tf_op | source)
XLA Modules:
  0.0 1316.6 jit_solution(13449929627954015853)
XLA Ops:
  1.9 2.0 fusion.356
  12.8 47.1 %custom-call.23 = f32[1,4,128,128]{3,2,1,0:T(8,128)S(1)} custom-call(f32[1,4,128,128]{3,2,1,0:T(8,128)S(1)} %cholesky.281), custom_call_target="Cholesky" | custom-call | tf_op jit(solution)/shard_map/jit(cholesky)/cholesky | solution.py:65
  60.0 39.3 %custom-call.24 = f32[1,4,1,128,128]{3,4,2,1,0:T(8,128)S(1)} custom-call(f32[1,4,1,128,128]{4,3,2,1,0:T(8,128)S(1)} %select_bitcast_fusion.2), custom_call_target="InvertDiagBlocksLowerTriangular" | custom-call | tf_op jit(solution)/shard_map/jit(cholesky)/cholesky | solution.py:65
  102.4 46.9 %custom-call.25 = f32[1,4,128,128]{3,2,1,0:T(8,128)S(1)} custom-call(f32[1,4,128,128]{3,2,1,0:T(8,128)S(1)} %fusion.25), custom_call_target="Cholesky" | custom-call | tf_op jit(solution)/shard_map/jit(cholesky)/cholesky | solution.py:65
  149.9 4.1 while.6
  154.0 78.8 %custom-call.26 = f32[4,2,128,128]{2,3,1,0:T(8,128)S(1)} custom-call(f32[4,2,128,128]{3,2,1,0:T(8,128)S(1)} %bitcast.916), custom_call_target="InvertDiagBlocksLowerTriangular" | custom-call | tf_op jit(solution)/shard_map/jit(_cho_solve)/vmap()/triangular_solve | solution.py:66
  243.4 2.2 fusion.42
  246.6 2.5 copy.272
  251.9 47.3 %custom-call.27 = f32[1,4,128,128]{3,2,1,0:T(8,128)S(1)} custom-call(f32[1,4,128,128]{3,2,1,0:T(8,128)S(1)} %cholesky.284), custom_call_target="Cholesky" | custom-call | tf_op jit(solution)/shard_map/jit(cholesky)/cholesky | solution.py:65
  301.7 40.7 %custom-call.28 = f32[1,4,1,128,128]{3,4,2,1,0:T(8,128)} custom-call(f32[1,4,1,128,128]{4,3,2,1,0:T(8,128)} %select_bitcast_fusion.1), custom_call_target="InvertDiagBlocksLowerTriangular" | custom-call | tf_op jit(solution)/shard_map/jit(cholesky)/cholesky | solution.py:65
  343.8 2.3 fusion.26
  346.2 48.3 %custom-call.29 = f32[1,4,128,128]{3,2,1,0:T(8,128)} custom-call(f32[1,4,128,128]{3,2,1,0:T(8,128)} %fusion.26), custom_call_target="Cholesky" | custom-call | tf_op jit(solution)/shard_map/jit(cholesky)/cholesky | solution.py:65
  398.9 5.2 while.7
  399.5 2.0 bitcast_dynamic-update-slice_fusion.10
  402.1 2.0 bitcast_dynamic-update-slice_fusion.10
  404.1 80.2 %custom-call.30 = f32[4,2,128,128]{2,3,1,0:T(8,128)} custom-call(f32[4,2,128,128]{3,2,1,0:T(8,128)} %bitcast.917), custom_call_target="InvertDiagBlocksLowerTriangular" | custom-call | tf_op jit(solution)/shard_map/jit(_cho_solve)/vmap()/triangular_solve | solution.py:66
  502.9 3.2 fusion.40
  506.1 2.1 fusion.48
  518.5 47.3 %custom-call.31 = f32[1,4,128,128]{3,2,1,0:T(8,128)S(1)} custom-call(f32[1,4,128,128]{3,2,1,0:T(8,128)S(1)} %cholesky.287), custom_call_target="Cholesky" | custom-call | tf_op jit(solution)/shard_map/jit(cholesky)/cholesky | solution.py:65
  568.3 40.7 %custom-call.32 = f32[1,4,1,128,128]{3,4,2,1,0:T(8,128)} custom-call(f32[1,4,1,128,128]{4,3,2,1,0:T(8,128)} %select_bitcast_fusion), custom_call_target="InvertDiagBlocksLowerTriangular" | custom-call | tf_op jit(solution)/shard_map/jit(cholesky)/cholesky | solution.py:65
  610.4 2.3 fusion.27
  612.8 48.3 %custom-call.33 = f32[1,4,128,128]{3,2,1,0:T(8,128)} custom-call(f32[1,4,128,128]{3,2,1,0:T(8,128)} %fusion.27), custom_call_target="Cholesky" | custom-call | tf_op jit(solution)/shard_map/jit(cholesky)/cholesky | solution.py:65
  665.4 5.4 while.8
  666.0 2.1 bitcast_dynamic-update-slice_fusion.11
  668.7 2.1 bitcast_dynamic-update-slice_fusion.11
  670.8 80.2 %custom-call.34 = f32[4,2,128,128]{2,3,1,0:T(8,128)} custom-call(f32[4,2,128,128]{3,2,1,0:T(8,128)} %bitcast.915), custom_call_target="InvertDiagBlocksLowerTriangular" | custom-call | tf_op jit(solution)/shard_map/jit(_cho_solve)/vmap()/triangular_solve | solution.py:66
  799.9 2.0 fusion.32
  802.6 2.1 fusion.97
  804.6 2.2 fusion.17
  808.6 2.0 fusion.33
  810.6 2.4 fusion.93
  817.9 2.4 fusion.370
  820.3 2.1 fusion.162
  833.0 2.3 convolution_subtract_fusion.7
  837.1 2.1 fusion.30
  846.8 2.2 fusion.31
  860.8 2.1 convert_bitcast_fusion.5
  862.9 2.0 convert_bitcast_fusion.4
  870.3 76.9 %all_to_all.5 = bf16[4,1,4,2,3,2,128,128]{7,6,5,4,3,2,1,0:T(8,128)(2,1)} all-to-all(bf16[4,1,4,2,3,2,128,128]{7,6,5,4,3,2,1,0:T(8,128)(2,1)S(1)} %stack.149), channel_id=1, replica_groups=mesh['kz'=4,'en'=32] {'kz'}, dimensions={0} | all-to-all | bytes 12582912 | tf_op jit(solution)/shard_map/all_to_all | solution.py:12
  947.2 5.2 collective-permute-start
  962.4 121.3 %collective-permute-done = bf16[4,4,2,3,2,128,128]{6,5,4,3,2,1,0:T(8,128)(2,1)} collective-permute-done((bf16[4,4,2,3,2,128,128]{6,5,4,3,2,1,0:T(8,128)(2,1)}, bf16[4,4,2,3,2,128,128]{6,5,4,3,2,1,0:T(8,128)(2,1)}, u32[]{:S(2)}, u32[]{:S(2)}) %collective-permute-start) | collective-permute-done | bytes 6291488 | tf_op jit(solution)/shard_map/ppermute | solution.py:20
  1083.7 137.4 %collective-permute-done.1 = bf16[4,4,2,3,2,128,128]{6,5,4,3,2,1,0:T(8,128)(2,1)} collective-permute-done((bf16[4,4,2,3,2,128,128]{6,5,4,3,2,1,0:T(8,128)(2,1)}, bf16[4,4,2,3,2,128,128]{6,5,4,3,2,1,0:T(8,128)(2,1)}, u32[]{:S(2)}, u32[]{:S(2)}) %collective-permute-start.1) | collective-permute-done | bytes 6291488 | tf_op jit(solution)/shard_map/ppermute | solution.py:23
  1221.2 15.0 %pad_maximum_fusion = bf16[4,12,2,3,2,128,128]{6,5,4,3,2,1,0:T(8,128)(2,1)} fusion(bf16[4,4,2,3,2,128,128]{6,5,4,3,2,1,0:T(8,128)(2,1)} %collective-permute-done.1, bf16[4,4,2,3,2,128,128]{6,5,4,3,2,1,0:T(8,128)(2,1)} %bitcast.201, bf16[4,4,2,3,2,128,128]{6,5,4,3,2,1,0:T(8,128)(2,1)} %collective-permute-done), kind=kLoop, calls=%fused_computation.6 | loop fusion | flops 18874368 | bytes 37748736 | tf_op jit(solution)/shard_map/concatenate | solution.py:24
  1236.2 17.9 %add_bitcast_fusion.1 = (f32[4,4,3,2,128,128]{5,4,3,2,1,0:T(8,128)}, f32[4,4,3,2,128,128]{5,4,3,2,1,0:T(8,128)}, f32[4,4,3,2,128,128]{5,4,3,2,1,0:T(8,128)S(1)}, f32[4,4,3,2,128,128]{5,4,3,2,1,0:T(8,128)}) fusion(bf16[4,12,2,3,2,128,128]{6,5,4,3,2,1,0:T(8,128)(2,1)} %pad_maximum_fusion, s32[]{:T(128)S(6)} %select_n.19, s32[]{:T(128)S(6)} %add.377, ...), kind=kLoop, calls=%fused_computation.16 | loop fusion | flops 31457280 | bytes 50331684 | tf_op jit(solution)/shard_map/add | solution.py:158
  1254.2 19.0 %fusion.6 = f32[1,4,3,2,128,128]{5,0,4,3,2,1:T(1,128)S(1)} fusion(f32[4,4,3,2,128,128]{5,4,3,2,1,0:T(8,128)} %get-tuple-element.68, f32[2,4]{1,0:T(2,128)S(1)} %fusion.36), kind=kOutput, calls=%fused_computation.13 | convolution fusion | flops 18874368 | bytes 7864832 | tf_op jit(solution)/shard_map/ak,kesrij->aesrij/dot_general | solution.py:161
  1273.2 13.8 %fusion.4 = f32[1,4,3,2,128,128]{5,0,4,3,2,1:T(1,128)S(1)} fusion(f32[4,4,3,2,128,128]{5,4,3,2,1,0:T(8,128)S(1)} %copy-done.3, f32[2,4]{1,0:T(2,128)S(1)} %fusion.36), kind=kOutput, calls=%fused_computation.11 | convolution fusion | flops 18874368 | bytes 7864832 | tf_op jit(solution)/shard_map/ak,kesrij->aesrij/dot_general | solution.py:161
  1287.0 13.6 %fusion.2 = f32[1,4,3,2,128,128]{5,0,4,3,2,1:T(1,128)S(1)} fusion(f32[4,4,3,2,128,128]{5,4,3,2,1,0:T(8,128)S(1)} %bitcast.901, f32[2,4]{1,0:T(2,128)S(1)} %fusion.36), kind=kOutput, calls=%fused_computation.9 | convolution fusion | flops 18874368 | bytes 7864832 | tf_op jit(solution)/shard_map/ak,kesrij->aesrij/dot_general | solution.py:164
  1300.7 13.8 %fusion = f32[1,4,3,2,128,128]{5,0,4,3,2,1:T(1,128)S(1)} fusion(f32[4,4,3,2,128,128]{5,4,3,2,1,0:T(8,128)S(1)} %get-tuple-element.67, f32[2,4]{1,0:T(2,128)S(1)} %fusion.36), kind=kOutput, calls=%fused_computation.7 | convolution fusion | flops 18874368 | bytes 7864832 | tf_op jit(solution)/shard_map/ak,kesrij->aesrij/dot_general | solution.py:164
  (347 shorter events, 177.0 us)
Async XLA Ops:
  9.2 50.7 %copy-start.52 = (pred[128,128]{1,0:T(8,128)(4,1)S(1)}, pred[128,128]{1,0:T(8,128)(4,1)}, u32[]{:S(2)}) copy-start(pred[128,128]{1,0:T(8,128)(4,1)} %iota_compare_fusion.1) | copy-start | bytes 49156
  11.3 138.5 %copy-start.62 = (s32[2]{0:T(128)S(1)}, s32[2]{0:T(128)}, u32[]{:S(2)}) copy-start(s32[2]{0:T(128)} %iota_multiply_fusion) | copy-start | bytes 28
  149.9 87.2 %copy-start.2 = (f32[2,128,128]{2,1,0:T(8,128)S(1)}, f32[2,128,128]{2,1,0:T(8,128)}, u32[]{:S(2)}) copy-start(f32[2,128,128]{2,1,0:T(8,128)} %param.18) | copy-start | bytes 393220
  154.0 83.7 %copy-start.60 = (s32[2,2]{1,0:T(2,128)}, s32[2,2]{1,0:T(2,128)S(1)}, u32[]{:S(2)}) copy-start(s32[2,2]{1,0:T(2,128)S(1)} %get-tuple-element.250) | copy-start | bytes 52
  240.8 10.0 copy-start.24
  242.3 57.6 %copy-start.53 = (pred[128,128]{1,0:T(8,128)(4,1)S(1)}, pred[128,128]{1,0:T(8,128)(4,1)}, u32[]{:S(2)}) copy-start(pred[128,128]{1,0:T(8,128)(4,1)} %iota_compare_fusion.1) | copy-start | bytes 49156
  246.6 152.3 %copy-start.61 = (s32[2,2]{1,0:T(2,128)S(1)}, s32[2,2]{1,0:T(2,128)}, u32[]{:S(2)}) copy-start(s32[2,2]{1,0:T(2,128)} %copy-done.60) | copy-start | bytes 52
  488.2 13.3 %copy-start.56 = (f32[4]{0:T(128)S(1)}, f32[4]{0:T(128)}, u32[]{:S(2)}) copy-start(f32[4]{0:T(128)} %copy-done.55) | copy-start | bytes 52
  493.7 16.6 %copy-start.36 = (bf16[1,4,2,128,128]{4,3,1,2,0:T(8,128)(2,1)S(1)}, bf16[1,4,2,128,128]{4,3,1,2,0:T(8,128)(2,1)}, u32[]{:S(2)}) copy-start(bf16[1,4,2,128,128]{4,3,1,2,0:T(8,128)(2,1)} %get-tuple-element.88) | copy-start | bytes 786436
  497.7 15.5 %copy-start.26 = (f32[1,4,2,128,128]{3,4,1,2,0:T(8,128)}, f32[1,4,2,128,128]{3,4,1,2,0:T(8,128)S(1)}, u32[]{:S(2)}) copy-start(f32[1,4,2,128,128]{3,4,1,2,0:T(8,128)S(1)} %get-tuple-element.113) | copy-start | bytes 1572868
  751.0 7.4 copy-start.43
  751.0 10.8 copy-start.37
  751.0 10.8 copy-start.45
  752.9 9.3 copy-start.48
  754.6 8.7 copy-start.25
  756.2 8.1 copy-start.47
  762.1 8.8 copy-start.27
  762.8 7.7 copy-start.7
  765.0 26.9 %copy-start.9 = (f32[4,128,128]{1,2,0:T(8,128)}, f32[4,128,128]{1,2,0:T(8,128)S(1)}, u32[]{:S(2)}) copy-start(f32[4,128,128]{1,2,0:T(8,128)S(1)} %convolution_subtract_fusion.24) | copy-start | bytes 786436
  767.1 9.2 copy-start.16
  769.8 9.2 copy-start.15
  770.5 24.3 %copy-start.13 = (f32[4,128,128]{1,2,0:T(8,128)}, f32[4,128,128]{1,2,0:T(8,128)S(1)}, u32[]{:S(2)}) copy-start(f32[4,128,128]{1,2,0:T(8,128)S(1)} %convolution_add_fusion.13) | copy-start | bytes 786436
  770.9 9.5 copy-start.4
  776.3 13.7 %copy-start.5 = (f32[4,128,128]{2,1,0:T(8,128)}, f32[4,128,128]{2,1,0:T(8,128)S(1)}, u32[]{:S(2)}) copy-start(f32[4,128,128]{2,1,0:T(8,128)S(1)} %fusion.174) | copy-start | bytes 786436
  780.4 10.6 copy-start.14
  781.5 10.3 copy-start.17
  787.1 9.1 copy-start.20
  788.7 7.5 copy-start.22
  789.6 6.6 copy-start.19
  808.6 13.8 %copy-start.31 = (f32[1,4,128,128]{3,2,1,0:T(8,128)S(1)}, f32[1,4,128,128]{3,2,1,0:T(8,128)}, u32[]{:S(2)}) copy-start(f32[1,4,128,128]{3,2,1,0:T(8,128)} %copy-done.30) | copy-start | bytes 786436
  810.6 22.3 %copy-start.8 = (f32[4,128,128]{1,2,0:T(8,128)S(1)}, f32[4,128,128]{1,2,0:T(8,128)}, u32[]{:S(2)}) copy-start(f32[4,128,128]{1,2,0:T(8,128)} %copy-done.7) | copy-start | bytes 786436
  814.8 26.2 %copy-start.21 = (f32[4,128,128]{2,1,0:T(8,128)S(1)}, f32[4,128,128]{2,1,0:T(8,128)}, u32[]{:S(2)}) copy-start(f32[4,128,128]{2,1,0:T(8,128)} %copy-done.20) | copy-start | bytes 786436
  816.6 27.0 %copy-start.10 = (f32[4,128,128]{1,2,0:T(8,128)S(1)}, f32[4,128,128]{1,2,0:T(8,128)}, u32[]{:S(2)}) copy-start(f32[4,128,128]{1,2,0:T(8,128)} %copy-done.9) | copy-start | bytes 786436
  828.5 28.4 %copy-start.12 = (f32[1,4,128,128]{3,2,1,0:T(8,128)S(1)}, f32[1,4,128,128]{3,2,1,0:T(8,128)}, u32[]{:S(2)}) copy-start(f32[1,4,128,128]{3,2,1,0:T(8,128)} %copy-done.11) | copy-start | bytes 786436
  843.5 22.5 %copy-start.50 = (bf16[1,4,1,128,128]{3,4,1,2,0:T(8,128)(2,1)S(1)}, bf16[1,4,1,128,128]{3,4,1,2,0:T(8,128)(2,1)}, u32[]{:S(2)}) copy-start(bf16[1,4,1,128,128]{3,4,1,2,0:T(8,128)(2,1)} %convert_bitcast_fusion) | copy-start | bytes 393220
  846.8 20.2 %copy-start.18 = (f32[4,128,128]{1,2,0:T(8,128)S(1)}, f32[4,128,128]{1,2,0:T(8,128)}, u32[]{:S(2)}) copy-start(f32[4,128,128]{1,2,0:T(8,128)} %copy-done.17) | copy-start | bytes 786436
  860.8 6.2 copy-start.51
  860.8 6.2 copy-start.49
  870.2 83.5 %copy-start.57 = (s32[2]{0:T(128)S(1)}, s32[2]{0:T(128)}, u32[]{:S(2)}) copy-start(s32[2]{0:T(128)} %param.24) | copy-start | bytes 28
  870.2 89.3 %copy-start.58 = (f32[2]{0:T(128)S(1)}, f32[2]{0:T(128)}, u32[]{:S(2)}) copy-start(f32[2]{0:T(128)} %param.23) | copy-start | bytes 28
  870.2 92.0 %copy-start.59 = (f32[2,4]{1,0:T(2,128)S(1)}, f32[2,4]{1,0:T(2,128)}, u32[]{:S(2)}) copy-start(f32[2,4]{1,0:T(2,128)} %param.21) | copy-start | bytes 100
  870.2 92.2 %copy-start.54 = (f32[2,128,128]{2,1,0:T(8,128)S(1)}, f32[2,128,128]{2,1,0:T(8,128)}, u32[]{:S(2)}) copy-start(f32[2,128,128]{2,1,0:T(8,128)} %param.22) | copy-start | bytes 393220
  947.2 136.6 %collective-permute-start = (bf16[4,4,2,3,2,128,128]{6,5,4,3,2,1,0:T(8,128)(2,1)}, bf16[4,4,2,3,2,128,128]{6,5,4,3,2,1,0:T(8,128)(2,1)}, u32[]{:S(2)}, u32[]{:S(2)}) collective-permute-start(bf16[4,4,2,3,2,128,128]{6,5,4,3,2,1,0:T(8,128)(2,1)} %bitcast.201), channel_id=1, source_target_pairs={{0,1},{1,2},{2,3},{3,4},{4,5},{5,6},{6,7},{7,8},{8,9},{9,10},{10,1... | collective-permute-start | bytes 18874376 | tf_op jit(solution)/shard_map/ppermute | solution.py:20
  952.4 268.8 %collective-permute-start.1 = (bf16[4,4,2,3,2,128,128]{6,5,4,3,2,1,0:T(8,128)(2,1)}, bf16[4,4,2,3,2,128,128]{6,5,4,3,2,1,0:T(8,128)(2,1)}, u32[]{:S(2)}, u32[]{:S(2)}) collective-permute-start(bf16[4,4,2,3,2,128,128]{6,5,4,3,2,1,0:T(8,128)(2,1)} %bitcast.201), channel_id=1, source_target_pairs={{1,0},{2,1},{3,2},{4,3},{5,4},{6,5},{7,6},{8,7},{9,8},{10,9},{11,1... | collective-permute-start | bytes 18874376 | tf_op jit(solution)/shard_map/ppermute | solution.py:23
  1254.2 19.0 %copy-start.3 = (f32[4,4,3,2,128,128]{5,4,3,2,1,0:T(8,128)S(1)}, f32[4,4,3,2,128,128]{5,4,3,2,1,0:T(8,128)}, u32[]{:S(2)}) copy-start(f32[4,4,3,2,128,128]{5,4,3,2,1,0:T(8,128)} %get-tuple-element.66) | copy-start | bytes 18874372
  1254.2 32.8 %slice-start = ((s8[6291456]{0:T(1024)(128)(4,1)}), s8[4194304]{0:T(1024)(128)(4,1)S(1)}, s32[]{:S(2)}) async-start(s8[6291456]{0:T(1024)(128)(4,1)} %bitcast.900), calls=%async_computation.1 | async-start | bytes 8388608
  1273.2 13.9 %slice-start.1 = ((s8[6291456]{0:T(1024)(128)(4,1)}), s8[2097152]{0:T(1024)(128)(4,1)S(1)}, s32[]{:S(2)}) async-start(s8[6291456]{0:T(1024)(128)(4,1)} %bitcast.900), calls=%async_computation.2 | async-start | bytes 4194304
  1300.7 15.7 %copy-start.1 = (f32[3,128,128]{2,1,0:T(8,128)S(1)}, f32[3,128,128]{2,1,0:T(8,128)}, u32[]{:S(2)}) copy-start(f32[3,128,128]{2,1,0:T(8,128)} %param.16) | copy-start | bytes 589828
  (19 other events, 42.8 us)
